TPU v7x, 32 devices: a whole 2x2x4 slice. The times are simulated.
32 devices in a mesh: dp: 8 (over z, x), expert: 4 (over y, core).
Axes of the slice: x: 2, y: 2, z: 4, core: 2. Of those that a mesh axis runs over, the one named last changes fastest.
Arguments:
- hidden: bfloat16 [2048, 2304], P(('dp', 'expert')), may hold values from -6 to 6
- tree_qkv: bfloat16 [2048, 6912], P(('dp', 'expert')), may hold values from -7 to 7
- prompt_kv: bfloat16 [8, 512, 4608], P('dp', 'expert'), may hold values from -6 to 6
- prompt_len: int32 [8], P('dp'), may hold values from 128 to 512, as said below
- private_kv: bfloat16 [32, 512, 4608], P(('dp', 'expert')), may hold values from -6 to 6
- priv_len: int32 [32], P(('dp', 'expert')), may hold values from 1 to 512, as said below
- parents: int32 [32, 64], P(('dp', 'expert')), may hold values from -1 to 62, as said below
- leaf: int32 [32], P(('dp', 'expert')), may hold values from 0 to 63
- w_out: bfloat16 [2304, 2304], replicated, may hold values from -3 to 3
- norm_gain: float32 [2304], replicated, may hold values from 0.1 to 1.9
- w_router: bfloat16 [2304, 4], replicated, as said below
- routes: int32 [2048, 2], P(('dp', 'expert')), may hold values from 0 to 3, all different within a row; in each aligned block of 64 rows (0 to 63, 64 to 127, ...) at most 48 rows name the same one
- w_gate_up: bfloat16 [4, 2, 2304, 5760], P('expert', None, None, 'dp'), may hold values from -0.125 to 0.125
- w_down: bfloat16 [4, 5760, 2304], P('expert', 'dp'), may hold values from -0.15625 to 0.15625
Outputs:
- layer_out: bfloat16 [2048, 2304], P(('dp', 'expert'))
- accepted_kv: bfloat16 [32, 64, 4608], P(('dp', 'expert'))
Inputs may be any that keep to these rules, and one draw needn't show every extreme that they name: `routes`: the rows of one device (aligned blocks of 64 rows) name each expert at most 48 times; the two experts of a row differ. `prompt_len`: some group's length is exactly 512. `priv_len`: some request's length is exactly 512. parents[r, 0] = -1; for t >= 1, max(0, t - 8) <= parents[r, t] <= t - 1. `w_router`: entries lie within 3 / sqrt(27648) of zero.
All inputs are finite; a program needn't handle non-finite values.
Results may differ from a plain program's by a relative error of at most 0.014.
Values may be sent and summed in bfloat16 or wider, within the bound.
No kernel may reach another device: no remote copies, remote signals or barrier semaphores. Data moves between devices by JAX's collectives and lax.ppermute only.
A program may use at most 128 MiB of HBM per device.

v0:
```python
import math
import jax
import jax.numpy as jnp
from jax import lax
from jax.sharding import PartitionSpec as P

H = 36
HD = 64
TREE = 64
REQ_DEV = 1
NEG = -1e30
EPS = 1e-05
HIGH = lax.Precision.HIGHEST


def closure(parents):
    count = parents.shape[-1]
    columns = jnp.arange(count, dtype=jnp.int32)
    reached = (parents[:, :, None] == columns[None, None, :]).astype(jnp.float32) + jnp.eye(
        count, dtype=jnp.float32
    )[None]
    for sweeps in range((count - 1).bit_length()):
        reached = jnp.minimum(jnp.einsum("rij,rjk->rik", reached, reached, precision=HIGH), 1.0)
    return reached


def compact(reach_one, leaf_one, kv_one):
    count = reach_one.shape[0]
    marked = jnp.sum(
        jnp.where(jnp.arange(count, dtype=jnp.int32)[:, None] == leaf_one, reach_one, 0.0), axis=0
    )
    earlier = (
        jnp.arange(count, dtype=jnp.int32)[None, :] < jnp.arange(count, dtype=jnp.int32)[:, None]
    ).astype(jnp.float32)
    ordinal = jnp.dot(earlier, marked, precision=HIGH)
    slot_ids = jnp.arange(count, dtype=jnp.int32).astype(jnp.float32)
    chosen = jnp.where(slot_ids[:, None] == ordinal[None, :], marked[None, :], 0.0)
    return jnp.dot(chosen.astype(jnp.bfloat16), kv_one, preferred_element_type=jnp.float32).astype(
        jnp.bfloat16
    )


def partial_attention(query_matrix_rows, cache_rows, allowed):
    features = cache_rows.shape[1] // 2
    slots = cache_rows.shape[0]
    key_matrix_rows = cache_rows[:, :features].reshape(slots, H, HD)
    value_matrix_rows = cache_rows[:, features:].reshape(slots, H, HD)
    attention_score_scale = 1.0 / math.sqrt(HD)
    attention_scores = (
        jnp.einsum(
            "was,zas->waz", query_matrix_rows, key_matrix_rows, preferred_element_type=jnp.float32
        )
        * attention_score_scale
    )
    widened = allowed[:, None, :]
    attention_scores = jnp.where(widened, attention_scores, NEG)
    maxima = jnp.max(attention_scores, axis=-1)
    attention_weights = jnp.where(widened, jnp.exp(attention_scores - maxima[..., None]), 0.0)
    totals = jnp.sum(attention_weights, axis=-1)
    weighted_sum = jnp.einsum(
        "ubj,jbx->ubx",
        attention_weights.astype(jnp.bfloat16),
        value_matrix_rows,
        preferred_element_type=jnp.float32,
    )
    return (maxima, totals, weighted_sum)


def join_parts(first_part, second_part):
    highest = jnp.maximum(first_part[0], second_part[0])
    scale_first = jnp.exp(first_part[0] - highest)
    scale_second = jnp.exp(second_part[0] - highest)
    totals = first_part[1] * scale_first + second_part[1] * scale_second
    weighted_sum = first_part[2] * scale_first[..., None] + second_part[2] * scale_second[..., None]
    return (highest, totals, weighted_sum)


def as_rows(part_state, row_count):
    return (
        part_state[0].reshape(row_count, H),
        part_state[1].reshape(row_count, H),
        part_state[2].reshape(row_count, H, HD),
    )


def local(
    hidden,
    tree_qkv,
    prompt_kv,
    prompt_len,
    private_kv,
    priv_len,
    parents,
    leaf,
    w_out,
    norm_gain,
    w_router,
    routes,
    w_gate_up,
    w_down,
):
    row_count = hidden.shape[0]
    features = hidden.shape[1]
    query_vectors = tree_qkv[:, :features].reshape(row_count, H, HD)
    new_kv = tree_qkv[:, features:]
    reached = closure(parents)
    grouped_q = query_vectors.reshape(REQ_DEV, TREE, H, HD)
    grouped_kv = new_kv.reshape(REQ_DEV, TREE, 2 * features)
    tree_part = jax.vmap(partial_attention)(grouped_q, grouped_kv, reached > 0.5)
    private_slots = jnp.arange(private_kv.shape[1], dtype=jnp.int32)
    private_ok = jnp.broadcast_to(
        (private_slots[None, :] < priv_len[:, None])[:, None, :],
        (REQ_DEV, TREE, private_kv.shape[1]),
    )
    private_part = jax.vmap(partial_attention)(grouped_q, private_kv, private_ok)
    local_state = join_parts(as_rows(tree_part, row_count), as_rows(private_part, row_count))
    prompt_limit = prompt_len[0]
    start_state = (
        jnp.full((row_count, H), NEG, jnp.float32),
        jnp.zeros((row_count, H), jnp.float32),
        jnp.zeros((row_count, H, HD), jnp.float32),
    )
    shard_rows = lax.all_gather(prompt_kv, "expert", axis=1, tiled=True)
    piece_len = shard_rows.shape[1]
    places = jnp.arange(piece_len, dtype=jnp.int32)
    allowed = jnp.broadcast_to((places < prompt_limit)[None, :], (row_count, piece_len))
    prompt_state = join_parts(start_state, partial_attention(query_vectors, shard_rows[0], allowed))
    final_state = join_parts(local_state, prompt_state)
    context = (
        (final_state[2] / final_state[1][..., None])
        .reshape(row_count, features)
        .astype(jnp.bfloat16)
    )
    attended = jnp.dot(context, w_out, preferred_element_type=jnp.float32)
    middle = (hidden.astype(jnp.float32) + attended).astype(jnp.bfloat16)
    middle32 = middle.astype(jnp.float32)
    normed = (
        middle32 * lax.rsqrt(jnp.mean(middle32 * middle32, axis=1, keepdims=True) + EPS) * norm_gain
    ).astype(jnp.bfloat16)
    logits = jnp.dot(normed, w_router, preferred_element_type=jnp.float32)
    experts = w_router.shape[1]
    choose = routes[:, :, None] == jnp.arange(experts, dtype=jnp.int32)[None, None, :]
    picked = jnp.sum(jnp.where(choose, logits[:, None, :], 0.0), axis=2)
    gate_first = jax.nn.sigmoid(picked[:, 0] - picked[:, 1])
    gate_second = jax.nn.sigmoid(picked[:, 1] - picked[:, 0])
    capacity = 3 * row_count // experts
    onehot = choose.reshape(2 * row_count, experts).astype(jnp.float32)
    assign_ids = jnp.arange(2 * row_count, dtype=jnp.int32)
    earlier = (assign_ids[None, :] < assign_ids[:, None]).astype(jnp.float32)
    before = jnp.dot(earlier, onehot, precision=HIGH)
    slot_rank = jnp.sum(before * onehot, axis=1).astype(jnp.int32)
    target = routes.reshape(2 * row_count) * capacity + slot_rank
    select = (jnp.arange(experts * capacity, dtype=jnp.int32)[:, None] == target[None, :]).astype(
        jnp.bfloat16
    )
    doubled = jnp.repeat(normed, 2, axis=0)
    outgoing = (
        jnp.dot(select, doubled, preferred_element_type=jnp.float32)
        .astype(jnp.bfloat16)
        .reshape(experts, capacity, features)
    )
    gate_cols = w_gate_up[0, 0]
    up_cols = w_gate_up[0, 1]
    down_rows = w_down[0]
    arrived = lax.all_to_all(outgoing, "expert", split_axis=0, concat_axis=0, tiled=True)
    pooled = lax.all_gather(arrived.reshape(experts * capacity, features), "dp", axis=0, tiled=True)
    gate_act = jnp.dot(pooled, gate_cols, preferred_element_type=jnp.float32)
    upper = jnp.dot(pooled, up_cols, preferred_element_type=jnp.float32)
    hidden_units = (jax.nn.silu(gate_act) * upper).astype(jnp.bfloat16)
    summed_rows = lax.psum_scatter(
        jnp.dot(hidden_units, down_rows, preferred_element_type=jnp.float32).astype(jnp.bfloat16),
        "dp",
        scatter_dimension=0,
        tiled=True,
    ).astype(jnp.float32)
    returned = lax.all_to_all(
        summed_rows.reshape(experts, capacity, features).astype(jnp.bfloat16),
        "expert",
        split_axis=0,
        concat_axis=0,
        tiled=True,
    ).astype(jnp.float32)
    flat_back = returned.reshape(experts * capacity, features)
    fetched = jnp.take(flat_back, target, axis=0).reshape(row_count, 2, features)
    layer_out = (
        middle32 + gate_first[:, None] * fetched[:, 0] + gate_second[:, None] * fetched[:, 1]
    ).astype(jnp.bfloat16)
    accepted_kv = jax.vmap(compact)(reached, leaf, grouped_kv)
    return (layer_out, accepted_kv)


def solution(mesh):
    placed = (
        P(("dp", "expert"), None),
        P(("dp", "expert"), None),
        P("dp", "expert", None),
        P("dp"),
        P(("dp", "expert"), None, None),
        P(("dp", "expert")),
        P(("dp", "expert"), None),
        P(("dp", "expert")),
        P(),
        P(),
        P(),
        P(("dp", "expert"), None),
        P("expert", None, None, "dp"),
        P("expert", "dp", None),
    )
    return jax.shard_map(
        local,
        mesh=mesh,
        in_specs=placed,
        out_specs=(P(("dp", "expert"), None), P(("dp", "expert"), None, None)),
        check_vma=False,
    )
```

profile of v0, /device:TPU:0, one launch (start us, length us, event | category | flops | bytes accessed | tf_op | source)
XLA Modules:
  0.0 406.6 jit_solution(13038210003141550185)
XLA Ops:
  7.2 0.7 all-gather.3.cloned.1.call-update
  8.0 1.0 fusion.86
  10.1 1.7 slice.46
  11.8 2.3 reshape.469
  14.1 1.1 slice_bitcast_fusion.2
  15.2 0.9 fusion.112
  16.0 2.3 reshape.468
  19.0 5.4 %fusion.110 = (bf16[1,512,2304]{2,1,0:T(8,128)(2,1)}, bf16[1,512,2304]{2,1,0:T(8,128)(2,1)}) fusion(bf16[1,512,4608]{2,1,0:T(8,128)(2,1)} %param.18), kind=kLoop, calls=%fused_computation.152 | loop fusion | bytes 9437184 | tf_op jit(solution)/shard_map/vmap()/slice | solution.py:47
  24.4 4.3 %copy.66 = bf16[1,512,2304]{1,2,0:T(8,128)(2,1)} copy(bf16[1,512,2304]{2,1,0:T(8,128)(2,1)} %get-tuple-element.8) | data formatting | bytes 4718592 | tf_op jit(solution)/shard_map/vmap()/slice | solution.py:46
  29.4 4.3 %copy.68 = bf16[1,512,2304]{1,2,0:T(8,128)(2,1)} copy(bf16[1,512,2304]{2,1,0:T(8,128)(2,1)} %get-tuple-element.7) | data formatting | bytes 4718592 | tf_op jit(solution)/shard_map/vmap()/slice | solution.py:47
  33.7 2.3 reshape.471
  36.4 1.9 fusion.113
  38.3 0.3 fusion.65
  38.6 0.7 copy-done.11
  39.3 0.9 bitcast_reduce_fusion.1
  40.2 2.2 copy-done.2
  42.4 1.4 fusion.7
  43.8 5.9 %all-gather.3.cloned.1.call-done = bf16[1,512,4608]{2,1,0:T(8,128)(2,1)} async-done(((bf16[1,128,4608]{2,1,0:T(8,128)(2,1)}), bf16[1,512,4608]{2,1,0:T(8,128)(2,1)}) %all-gather.3.cloned.1.call-update) | async-done | bytes 4718608 | tf_op jit(solution)/shard_map/all_gather | solution.py:123
  49.7 4.9 %fusion.111 = (bf16[512,2304]{1,0:T(8,128)(2,1)}, bf16[512,2304]{1,0:T(8,128)(2,1)}) fusion(bf16[512,4608]{1,0:T(8,128)(2,1)} %bitcast.201), kind=kLoop, calls=%fused_computation.153 | loop fusion | bytes 9437184 | tf_op jit(solution)/shard_map/slice | solution.py:46
  54.6 4.3 %copy.69 = bf16[512,2304]{0,1:T(8,128)(2,1)} copy(bf16[512,2304]{1,0:T(8,128)(2,1)} %get-tuple-element.9) | data formatting | bytes 4718592 | tf_op jit(solution)/shard_map/slice | solution.py:46
  58.9 4.3 %copy.71 = bf16[512,2304]{0,1:T(8,128)(2,1)} copy(bf16[512,2304]{1,0:T(8,128)(2,1)} %get-tuple-element.10) | data formatting | bytes 4718592 | tf_op jit(solution)/shard_map/slice | solution.py:47
  63.2 2.9 bitcast_reduce_fusion
  66.0 1.5 fusion.9
  67.7 1.4 fusion.59
  69.1 0.3 copy-done.10
  69.4 1.9 fusion.56
  71.3 1.8 fusion.62
  73.0 1.2 copy.72
  74.3 2.2 convert_element_type.146
  76.4 6.1 %multiply_reduce_fusion = (f32[64]{0:T(128)S(1)}, f32[64,2304]{1,0:T(8,128)S(1)}) fusion(bf16[64,2304]{1,0:T(8,128)(2,1)} %convert_element_type.146, bf16[2304,2304]{1,0:T(8,128)(2,1)} %param.22, bf16[64,2304]{1,0:T(8,128)(2,1)} %param.14), kind=kOutput, calls=%fused_computation.86 | convolution fusion | flops 680361920 | bytes 11796736 | tf_op jit(solution)/shard_map/dot_general | solution.py:134
  82.6 0.8 copy-done.4
  83.5 0.7 copy-done.6
  84.2 1.1 broadcast_in_dim.163
  85.4 2.7 reshape.480
  88.1 1.4 convolution_convert_fusion.2
  89.5 15.8 %all_to_all.10 = bf16[4,48,2304]{2,1,0:T(8,128)(2,1)} all-to-all(bf16[4,48,2304]{2,1,0:T(8,128)(2,1)S(1)} %bitcast.203), channel_id=1, replica_groups=mesh['dp'=8,'expert'=4] {'expert'}, dimensions={0} | all-to-all | bytes 1769472 | tf_op jit(solution)/shard_map/all_to_all | solution.py:165
  105.4 108.4 %all-gather.5.cloned.1.call-done = bf16[1536,2304]{1,0:T(8,128)(2,1)} async-done(((bf16[192,2304]{1,0:T(8,128)(2,1)}), bf16[1536,2304]{1,0:T(8,128)(2,1)}) %all-gather.5.cloned.1.call-update) | async-done | bytes 7077904 | tf_op jit(solution)/shard_map/all_gather | solution.py:166
  213.8 10.5 %fusion.15 = f32[1536,720]{0,1:T(8,128)} fusion(bf16[1536,2304]{1,0:T(8,128)(2,1)} %all-gather.5.cloned.1.call-done, bf16[1,2,2304,720]{2,3,1,0:T(8,128)(2,1)} %param.26), kind=kOutput, calls=%fused_computation.25 | convolution fusion | flops 5096079360 | bytes 14819328 | tf_op jit(solution)/shard_map/dot_general | solution.py:167
  224.3 20.2 %convolution_convert_fusion = bf16[1536,2304]{1,0:T(8,128)(2,1)} fusion(bf16[1,720,2304]{2,1,0:T(8,128)(2,1)S(1)} %copy-done, f32[1536,720]{0,1:T(8,128)} %fusion.15, bf16[1536,2304]{1,0:T(8,128)(2,1)} %all-gather.5.cloned.1.call-done, bf16[1,2,2304,720]{2,3,1,0:T(8,128)(2,1)} %param.26), kind=kOutput, calls=%fused_computation.1 | convolution fusion | flops 10202333184 | bytes 25214976 | tf_op jit(solution)/shard_map/dot_general | solution.py:171
  245.8 1.2 fusion
  247.1 124.9 %reduce-scatter.2.cloned.1.call-done = bf16[192,2304]{1,0:T(8,128)(2,1)} async-done(((bf16[1536,2304]{1,0:T(8,128)(2,1)}), bf16[192,2304]{1,0:T(8,128)(2,1)}) %reduce-scatter.2.cloned.1.call-update) | async-done | bytes 884752 | tf_op jit(solution)/shard_map/reduce_scatter | solution.py:170
  371.9 3.5 all-to-all-start.1
  375.7 12.4 %all-to-all-done.1 = bf16[4,48,2304]{2,1,0:T(8,128)(2,1)S(1)} async-done(((bf16[4,48,2304]{2,1,0:T(8,128)(2,1)}), bf16[4,48,2304]{2,1,0:T(8,128)(2,1)S(1)}, u32[]{:S(2)}, u32[]{:S(2)}) %all-to-all-start.1) | async-done | bytes 884768 | tf_op jit(solution)/shard_map/all_to_all | solution.py:176
  388.1 1.4 bitcast_convert_fusion
  389.5 4.2 %gather_fusion = f32[128,2304]{1,0:T(8,128)} fusion(f32[192,2304]{1,0:T(8,128)} %bitcast_convert_fusion, s32[1024]{0:T(1024)S(1)} %pad_clamp_fusion), kind=kCustom, calls=%fused_computation | custom fusion | bytes 2359808 | tf_op jit(solution)/shard_map/jit(_take)/gather | solution.py:184
  393.7 2.9 gather.7
  396.6 1.4 copy_select_fusion
  398.0 2.0 fusion.71
  (71 shorter events, 2.9 us)
Async XLA Ops:
  7.2 217.1 %copy-start = (bf16[1,720,2304]{2,1,0:T(8,128)(2,1)S(1)}, bf16[1,720,2304]{2,1,0:T(8,128)(2,1)}, u32[]{:S(2)}) copy-start(bf16[1,720,2304]{2,1,0:T(8,128)(2,1)} %param.27) | copy-start | bytes 9953284
  7.2 42.6 %all-gather.3.cloned.1.call-start = ((), (), s32[]{:S(2)}) async-start(), calls=%async_computation.3 | async-start | bytes 5898240 | tf_op jit(solution)/shard_map/all_gather | solution.py:123
  7.9 205.9 %all-gather.5.cloned.1.call-start = ((), (), s32[]{:S(2)}) async-start(), calls=%async_computation.4 | async-start | bytes 7962624 | tf_op jit(solution)/shard_map/all_gather | solution.py:166
  28.7 7.2 %copy-start.15 = (s32[64,2]{0,1:T(2,128)S(1)}, s32[64,2]{0,1:T(2,128)}, u32[]{:S(2)}) copy-start(s32[64,2]{0,1:T(2,128)} %param.25) | copy-start | bytes 1540
  36.2 3.1 copy-start.3
  36.2 3.1 copy-start.5
  38.3 1.0 copy-start.11
  40.2 2.2 copy-start.2
  63.2 4.4 %slice-start = ((s8[4718592]{0:T(1024)(128)(4,1)}), s8[4194304]{0:T(1024)(128)(4,1)S(1)}, s32[]{:S(2)}) async-start(s8[4718592]{0:T(1024)(128)(4,1)} %bitcast.197), calls=%async_computation.6 | async-start | bytes 8388608
  63.2 4.4 %slice-start.1 = ((s8[4718592]{0:T(1024)(128)(4,1)}), s8[524288]{0:T(1024)(128)(4,1)S(1)}, s32[]{:S(2)}) async-start(s8[4718592]{0:T(1024)(128)(4,1)} %bitcast.197), calls=%async_computation.7 | async-start | bytes 1048576
  66.0 1.7 copy-start.9
  67.7 1.7 copy-start.10
  69.4 1.9 copy-start.12
  69.4 1.9 copy-start.13
  76.4 7.0 %copy-start.16 = (f32[2304]{0:T(1024)S(1)}, f32[2304]{0:T(1024)}, u32[]{:S(2)}) copy-start(f32[2304]{0:T(1024)} %param.23) | copy-start | bytes 27652
  82.6 0.8 copy-start.4
  83.5 0.7 copy-start.6
  105.4 266.6 %reduce-scatter.2.cloned.1.call-start = ((), (), s32[]{:S(2)}) async-start(), calls=%async_computation.5 | async-start | bytes 7962624 | tf_op jit(solution)/shard_map/reduce_scatter | solution.py:170
  244.4 1.4 copy-start.8
  244.4 131.0 %copy-start.7 = (bf16[64,2304]{1,0:T(8,128)(2,1)S(1)}, bf16[64,2304]{1,0:T(8,128)(2,1)}, u32[]{:S(2)}) copy-start(bf16[64,2304]{1,0:T(8,128)(2,1)} %copy-done.6) | copy-start | bytes 884740
  244.4 131.0 %copy-start.14 = (bf16[2304,4]{0,1:T(4,128)(2,1)S(1)}, bf16[2304,4]{0,1:T(4,128)(2,1)}, u32[]{:S(2)}) copy-start(bf16[2304,4]{0,1:T(4,128)(2,1)} %param.24) | copy-start | bytes 55300
  371.9 16.2 %all-to-all-start.1 = ((bf16[4,48,2304]{2,1,0:T(8,128)(2,1)}), bf16[4,48,2304]{2,1,0:T(8,128)(2,1)S(1)}, u32[]{:S(2)}, u32[]{:S(2)}) async-start(bf16[4,48,2304]{2,1,0:T(8,128)(2,1)} %bitcast.206), calls=%async_computation.2 | async-start | bytes 1769472 | tf_op jit(solution)/shard_map/all_to_all | solution.py:176
  389.5 10.5 %copy-start.1 = (bf16[1,720,2304]{2,1,0:T(8,128)(2,1)S(1)}, bf16[1,720,2304]{2,1,0:T(8,128)(2,1)}, u32[]{:S(2)}) copy-start(bf16[1,720,2304]{2,1,0:T(8,128)(2,1)} %param.27) | copy-start | bytes 9953284
Sparse Core Ops, SparseCore 0:
  9.5 40.1 all-gather.2
  105.5 108.2 all-gather.4
  244.6 127.3 reduce-scatter.1
where the time goes:
time: 408 us; the launch traced here: 407 us
  waiting for transfers between devices  252 us (62%)
  local copies, waits for them, and re-layouts  57.9 us (14%)
  matrix products  51.5 us (13%)
  between operations  16.1 us (4%)
  blocking collectives  15.8 us (4%)
  other arithmetic  9.36 us (2%)
    reduce_scatter x1, waiting for transfers between devices, local(): lax.psum_scatter(jnp.dot(hidden_units, down_rows, preferred_element_type=...  125 us
    all_gather x1, waiting for transfers between devices, local(): lax.all_gather(arrived.reshape(experts * capacity, features), 'dp', axis=...  108 us
    dot_general x1, matrix products, local(): jnp.dot(hidden_units, down_rows, preferred_element_type=jnp.float32)  20.2 us
    all_to_all x1, blocking collectives, local(): lax.all_to_all(outgoing, 'expert', split_axis=0, concat_axis=0, tiled=True)  15.8 us
    slice x4, local copies, waits for them, and re-layouts, partial_attention(): value_matrix_rows = cache_rows[:, features:].reshape(slots, H, HD)  14.8 us
    slice x3, local copies, waits for them, and re-layouts, partial_attention(): key_matrix_rows = cache_rows[:, :features].reshape(slots, H, HD)  13.4 us
    all_to_all x1, waiting for transfers between devices, local(): lax.all_to_all(summed_rows.reshape(experts, capacity, features).astype(jn...  12.4 us
    dot_general x1, matrix products, local(): gate_act = jnp.dot(pooled, gate_cols, preferred_element_type=jnp.float32)  10.5 us
  transfers between devices with their start and end apart: 4, of which 4 were waited for; matrix products, arithmetic and copies ran while one was open for 8% of the time, Pallas kernels for 0%

commit v1 on v0

--- a/solution.py
+++ b/solution.py
@@ -11,6 +11,24 @@
 NEG = -1e30
 EPS = 1e-05
 HIGH = lax.Precision.HIGHEST
+
+
+def joined_along(blocks, dim):
+    lengths = list(blocks.shape[1:])
+    lengths[dim] *= blocks.shape[0]
+    return jnp.moveaxis(blocks, 0, dim).reshape(lengths)
+
+
+def collected_by_bits(x, axis):
+    count = lax.axis_size(axis)
+    tiles = x[None]
+    for level in range(count.bit_length() - 1):
+        apart = 1 << level
+        theirs = lax.ppermute(tiles, axis, [(i, i ^ apart) for i in range(count)])
+        both = jnp.stack([tiles, theirs])
+        upper = lax.axis_index(axis) >> level & 1
+        tiles = jnp.where(upper == 0, both, both[::-1]).reshape(-1, *x.shape)
+    return tiles
 
 
 def closure(parents):
@@ -163,7 +181,8 @@
     up_cols = w_gate_up[0, 1]
     down_rows = w_down[0]
     arrived = lax.all_to_all(outgoing, "expert", split_axis=0, concat_axis=0, tiled=True)
-    pooled = lax.all_gather(arrived.reshape(experts * capacity, features), "dp", axis=0, tiled=True)
+    x = arrived.reshape(experts * capacity, features)
+    pooled = joined_along(collected_by_bits(x, "dp"), 0)
     gate_act = jnp.dot(pooled, gate_cols, preferred_element_type=jnp.float32)
     upper = jnp.dot(pooled, up_cols, preferred_element_type=jnp.float32)
     hidden_units = (jax.nn.silu(gate_act) * upper).astype(jnp.bfloat16)

time: 408 us -> 535 us (1.31)
  waiting for transfers between devices: 252 us -> 353 us
  other arithmetic: 9.36 us -> 26.9 us
  starting transfers between devices: 3.62 us -> 9.88 us
    ppermute x0 -> x3, waiting for transfers between devices: none -> 209 us  [collected_by_bits(): theirs = lax.ppermute(tiles, axis, [(i, i ^ apart) for i in range(count)])]
    all_gather x1 -> x0, waiting for transfers between devices: 108 us -> none  [local(): lax.all_gather(arrived.reshape(experts * capacity, features), 'dp', axis=...]
    another operation x0 -> x4, other arithmetic: none -> 9.76 us  [collected_by_bits(): both = jnp.stack([tiles, theirs])]
    select_n x0 -> x2, other arithmetic: none -> 6.72 us  [collected_by_bits(): tiles = jnp.where(upper == 0, both, both[::-1]).reshape(-1, *x.shape)]
    ppermute x0 -> x3, starting transfers between devices: none -> 5.37 us  [collected_by_bits(): theirs = lax.ppermute(tiles, axis, [(i, i ^ apart) for i in range(count)])]
  transfers between devices with their start and end apart: 4 -> 6, of which waited for: 4 -> 6; matrix products, arithmetic and copies ran while one was open for 8% -> 7% of each run, Pallas kernels for 0% -> 0%
where the time goes in v1:
time: 535 us; the launch traced here: 534 us
  waiting for transfers between devices  353 us (66%)
  local copies, waits for them, and re-layouts  57.7 us (11%)
  matrix products  53.5 us (10%)
  other arithmetic  26.9 us (5%)
  between operations  16.4 us (3%)
  blocking collectives  15.8 us (3%)
  starting transfers between devices  9.88 us (2%)
    ppermute x3, waiting for transfers between devices, collected_by_bits(): theirs = lax.ppermute(tiles, axis, [(i, i ^ apart) for i in range(count)])  209 us
    reduce_scatter x1, waiting for transfers between devices, local(): lax.psum_scatter(jnp.dot(hidden_units, down_rows, preferred_element_type=...  126 us
    dot_general x1, matrix products, local(): jnp.dot(hidden_units, down_rows, preferred_element_type=jnp.float32)  20.1 us
    all_to_all x1, blocking collectives, local(): lax.all_to_all(outgoing, 'expert', split_axis=0, concat_axis=0, tiled=True)  15.8 us
    slice x4, local copies, waits for them, and re-layouts, partial_attention(): value_matrix_rows = cache_rows[:, features:].reshape(slots, H, HD)  14.9 us
    slice x3, local copies, waits for them, and re-layouts, partial_attention(): key_matrix_rows = cache_rows[:, :features].reshape(slots, H, HD)  13.5 us
    all_to_all x1, waiting for transfers between devices, local(): lax.all_to_all(summed_rows.reshape(experts, capacity, features).astype(jn...  11.5 us
  transfers between devices with their start and end apart: 6, of which 6 were waited for; matrix products, arithmetic and copies ran while one was open for 7% of the time, Pallas kernels for 0%

profile of v1, /device:TPU:0, one launch (start us, length us, event | category | flops | bytes accessed | tf_op | source)
XLA Modules:
  0.0 533.7 jit_solution(3193009119544520275)
XLA Ops:
  10.1 1.7 slice.46
  11.8 2.3 reshape.472
  16.0 2.3 reshape.471
  19.0 5.4 %fusion.112 = (bf16[1,512,2304]{2,1,0:T(8,128)(2,1)}, bf16[1,512,2304]{2,1,0:T(8,128)(2,1)}) fusion(bf16[1,512,4608]{2,1,0:T(8,128)(2,1)} %param.18), kind=kLoop, calls=%fused_computation.160 | loop fusion | bytes 9437184 | tf_op jit(solution)/shard_map/vmap()/slice | solution.py:65
  24.4 4.3 copy.66
  29.4 4.3 copy.68
  33.7 2.3 reshape.474
  36.4 1.9 fusion.115
  40.2 2.2 copy-done.1
  42.4 1.4 fusion.7
  43.8 5.9 %all-gather.2.cloned.1.call-done = bf16[1,512,4608]{2,1,0:T(8,128)(2,1)} async-done(((bf16[1,128,4608]{2,1,0:T(8,128)(2,1)}), bf16[1,512,4608]{2,1,0:T(8,128)(2,1)}) %all-gather.2.cloned.1.call-update) | async-done | bytes 4718608 | tf_op jit(solution)/shard_map/all_gather | solution.py:141
  49.7 4.9 fusion.113
  54.6 4.3 copy.69
  58.9 4.3 copy.71
  63.2 2.9 bitcast_reduce_fusion
  66.1 1.5 fusion.9
  67.7 1.4 fusion.59
  69.4 1.9 fusion.56
  71.3 1.8 fusion.64
  73.1 1.2 copy.72
  74.3 2.2 convert_element_type.146
  76.5 6.1 %multiply_reduce_fusion = (f32[64]{0:T(128)S(1)}, f32[64,2304]{1,0:T(8,128)S(1)}) fusion(bf16[64,2304]{1,0:T(8,128)(2,1)} %convert_element_type.146, bf16[2304,2304]{1,0:T(8,128)(2,1)} %param.22, bf16[64,2304]{1,0:T(8,128)(2,1)} %param.14), kind=kOutput, calls=%fused_computation.94 | convolution fusion | flops 680361920 | bytes 11796736 | tf_op jit(solution)/shard_map/dot_general | solution.py:152
  85.4 2.7 reshape.483
  88.1 1.4 convolution_convert_fusion.2
  89.5 15.8 %all_to_all.10 = bf16[4,48,2304]{2,1,0:T(8,128)(2,1)} all-to-all(bf16[4,48,2304]{2,1,0:T(8,128)(2,1)S(1)} %bitcast.215), channel_id=1, replica_groups=mesh['dp'=8,'expert'=4] {'expert'}, dimensions={0} | all-to-all | bytes 1769472 | tf_op jit(solution)/shard_map/all_to_all | solution.py:183
  105.4 1.5 collective-permute-start
  106.8 20.0 %collective-permute-done = bf16[1,192,2304]{2,1,0:T(8,128)(2,1)} collective-permute-done((bf16[1,192,2304]{2,1,0:T(8,128)(2,1)}, bf16[1,192,2304]{2,1,0:T(8,128)(2,1)}, u32[]{:S(2)}, u32[]{:S(2)}) %collective-permute-start) | collective-permute-done | bytes 884768 | tf_op jit(solution)/shard_map/ppermute | solution.py:27
  126.8 1.6 pad_maximum_fusion.2
  128.4 2.1 fusion.63
  130.5 1.5 collective-permute-start.1
  132.0 38.1 %collective-permute-done.1 = bf16[2,192,2304]{2,1,0:T(8,128)(2,1)} collective-permute-done((bf16[2,192,2304]{2,1,0:T(8,128)(2,1)}, bf16[2,192,2304]{2,1,0:T(8,128)(2,1)}, u32[]{:S(2)}, u32[]{:S(2)}) %collective-permute-start.1) | collective-permute-done | bytes 1769504 | tf_op jit(solution)/shard_map/ppermute | solution.py:27
  170.1 2.3 pad_maximum_fusion.1
  172.4 2.4 reverse_select_fusion.1
  174.8 2.4 collective-permute-start.2
  177.2 150.9 %collective-permute-done.2 = bf16[4,192,2304]{2,1,0:T(8,128)(2,1)} collective-permute-done((bf16[4,192,2304]{2,1,0:T(8,128)(2,1)}, bf16[4,192,2304]{2,1,0:T(8,128)(2,1)}, u32[]{:S(2)}, u32[]{:S(2)}) %collective-permute-start.2) | collective-permute-done | bytes 3538976 | tf_op jit(solution)/shard_map/ppermute | solution.py:27
  328.2 3.7 pad_maximum_fusion
  331.9 4.3 reverse_select_fusion
  336.2 10.5 %fusion.15 = f32[1536,720]{0,1:T(8,128)} fusion(bf16[1536,2304]{1,0:T(8,128)(2,1)} %bitcast.212, bf16[1,2,2304,720]{2,3,1,0:T(8,128)(2,1)} %param.26), kind=kOutput, calls=%fused_computation.29 | convolution fusion | flops 5096079360 | bytes 14819328 | tf_op jit(solution)/shard_map/dot_general | solution.py:186
  346.7 20.1 %convolution_convert_fusion = bf16[1536,2304]{1,0:T(8,128)(2,1)} fusion(bf16[1,720,2304]{2,1,0:T(8,128)(2,1)S(1)} %copy-done, f32[1536,720]{0,1:T(8,128)} %fusion.15, bf16[1536,2304]{1,0:T(8,128)(2,1)} %bitcast.213, bf16[1,2,2304,720]{2,3,1,0:T(8,128)(2,1)} %param.26), kind=kOutput, calls=%fused_computation.1 | convolution fusion | flops 10202333184 | bytes 25214976 | tf_op jit(solution)/shard_map/dot_general | solution.py:190
  368.2 2.3 fusion
  370.5 126.3 %reduce-scatter.2.cloned.1.call-done = bf16[192,2304]{1,0:T(8,128)(2,1)} async-done(((bf16[1536,2304]{1,0:T(8,128)(2,1)}), bf16[192,2304]{1,0:T(8,128)(2,1)}) %reduce-scatter.2.cloned.1.call-update) | async-done | bytes 884752 | tf_op jit(solution)/shard_map/reduce_scatter | solution.py:189
  496.8 4.4 all-to-all-start.1
  502.5 11.5 %all-to-all-done.1 = bf16[4,48,2304]{2,1,0:T(8,128)(2,1)} async-done(((bf16[4,48,2304]{2,1,0:T(8,128)(2,1)}), bf16[4,48,2304]{2,1,0:T(8,128)(2,1)}, u32[]{:S(2)}, u32[]{:S(2)}) %all-to-all-start.1) | async-done | bytes 884768 | tf_op jit(solution)/shard_map/all_to_all | solution.py:195
  514.0 2.5 bitcast_convert_fusion
  516.5 4.0 gather_fusion
  520.5 2.9 gather.7
  523.5 1.4 copy_select_fusion
  524.9 2.0 fusion.73
  (74 shorter events, 12.2 us)
Async XLA Ops:
  7.2 339.5 %copy-start = (bf16[1,720,2304]{2,1,0:T(8,128)(2,1)S(1)}, bf16[1,720,2304]{2,1,0:T(8,128)(2,1)}, u32[]{:S(2)}) copy-start(bf16[1,720,2304]{2,1,0:T(8,128)(2,1)} %param.27) | copy-start | bytes 9953284
  7.2 42.6 %all-gather.2.cloned.1.call-start = ((), (), s32[]{:S(2)}) async-start(), calls=%async_computation.3 | async-start | bytes 5898240 | tf_op jit(solution)/shard_map/all_gather | solution.py:141
  7.9 488.9 %reduce-scatter.2.cloned.1.call-start = ((), (), s32[]{:S(2)}) async-start(), calls=%async_computation.4 | async-start | bytes 7962624 | tf_op jit(solution)/shard_map/reduce_scatter | solution.py:189
  28.7 7.2 %copy-start.12 = (s32[64,2]{0,1:T(2,128)S(1)}, s32[64,2]{0,1:T(2,128)}, u32[]{:S(2)}) copy-start(s32[64,2]{0,1:T(2,128)} %param.25) | copy-start | bytes 1540
  36.2 3.1 copy-start.2
  36.2 3.1 copy-start.4
  38.3 1.0 copy-start.8
  40.2 2.2 copy-start.1
  63.2 4.4 slice-start
  63.2 4.4 slice-start.1
  66.1 1.7 copy-start.6
  67.7 1.7 copy-start.7
  69.4 1.9 copy-start.9
  69.4 1.9 copy-start.10
  76.5 7.0 %copy-start.13 = (f32[2304]{0:T(1024)S(1)}, f32[2304]{0:T(1024)}, u32[]{:S(2)}) copy-start(f32[2304]{0:T(1024)} %param.23) | copy-start | bytes 27652
  82.6 0.8 copy-start.3
  83.6 0.7 copy-start.5
  105.4 21.5 %collective-permute-start = (bf16[1,192,2304]{2,1,0:T(8,128)(2,1)}, bf16[1,192,2304]{2,1,0:T(8,128)(2,1)}, u32[]{:S(2)}, u32[]{:S(2)}) collective-permute-start(bf16[1,192,2304]{2,1,0:T(8,128)(2,1)} %bitcast.29), channel_id=1, source_target_pairs={{0,4},{4,0},{8,12},{12,8},{16,20},{20,16},{24,28},{28,24},{1,5},{5... | collective-permute-start | bytes 2654216 | tf_op jit(solution)/shard_map/ppermute | solution.py:27
  130.5 39.6 %collective-permute-start.1 = (bf16[2,192,2304]{2,1,0:T(8,128)(2,1)}, bf16[2,192,2304]{2,1,0:T(8,128)(2,1)}, u32[]{:S(2)}, u32[]{:S(2)}) collective-permute-start(bf16[2,192,2304]{2,1,0:T(8,128)(2,1)} %get-tuple-element.12), channel_id=1, source_target_pairs={{0,8},{4,12},{8,0},{12,4},{16,24},{20,28},{24,16},{28,20},{1,9},{5... | collective-permute-start | bytes 5308424 | tf_op jit(solution)/shard_map/ppermute | solution.py:27
  174.8 153.4 %collective-permute-start.2 = (bf16[4,192,2304]{2,1,0:T(8,128)(2,1)}, bf16[4,192,2304]{2,1,0:T(8,128)(2,1)}, u32[]{:S(2)}, u32[]{:S(2)}) collective-permute-start(bf16[4,192,2304]{2,1,0:T(8,128)(2,1)} %bitcast.35), channel_id=1, source_target_pairs={{0,16},{4,20},{8,24},{12,28},{16,0},{20,4},{24,8},{28,12},{1,17},{... | collective-permute-start | bytes 10616840 | tf_op jit(solution)/shard_map/ppermute | solution.py:27
  366.8 134.5 %copy-start.11 = (bf16[2304,4]{0,1:T(4,128)(2,1)S(1)}, bf16[2304,4]{0,1:T(4,128)(2,1)}, u32[]{:S(2)}) copy-start(bf16[2304,4]{0,1:T(4,128)(2,1)} %param.24) | copy-start | bytes 55300
  496.8 17.2 %all-to-all-start.1 = ((bf16[4,48,2304]{2,1,0:T(8,128)(2,1)}), bf16[4,48,2304]{2,1,0:T(8,128)(2,1)}, u32[]{:S(2)}, u32[]{:S(2)}) async-start(bf16[4,48,2304]{2,1,0:T(8,128)(2,1)} %bitcast.218), calls=%async_computation.2 | async-start | bytes 1769472 | tf_op jit(solution)/shard_map/all_to_all | solution.py:195
Sparse Core Ops, SparseCore 0:
  9.5 40.1 all-gather.1
  366.9 129.8 reduce-scatter.1
